TPU v7x, 512 devices: a whole 4x4x16 slice. The times are simulated.
512 devices in a mesh: req: 32 (over y, x, core), mlp: 16 (over z).
Axes of the slice: x: 4, y: 4, z: 16, core: 2. Of those that a mesh axis runs over, the one named last changes fastest.
Arguments:
- queries: bfloat16 [12288, 4096], P('req', 'mlp')
- new_keys: bfloat16 [12288, 1024], P(('req', 'mlp')), may hold values from -5 to 5
- new_values: bfloat16 [12288, 1024], P(('req', 'mlp')), may hold values from -6 to 6
- cache_keys: bfloat16 [32, 4096, 1024], P('req', 'mlp')
- cache_values: bfloat16 [32, 4096, 1024], P('req', 'mlp'), may hold values from -6 to 6
- cache_len: int32 [32], P('req'), may hold values from 256 to 4096, as said below
- residual: bfloat16 [12288, 2560], P('req')
- out_weight: bfloat16 [4096, 2560], P('mlp'), may hold values from -0.1796875 to 0.1796875
- norm_gain: bfloat16 [2560], replicated, may hold values from 0.099609375 to 1.8984375
- gate_weight: bfloat16 [2560, 9728], P('req', 'mlp'), may hold values from -0.125 to 0.125
- up_weight: bfloat16 [2560, 9728], P('req', 'mlp'), may hold values from -0.125 to 0.125
- down_weight: bfloat16 [2560, 9728], P('req', 'mlp'), may hold values from -0.0625 to 0.0625
Outputs:
- layer_out: bfloat16 [12288, 2560], P(('req', 'mlp'))
Inputs may be any that keep to these rules, and one draw needn't show every extreme that they name: cache_len[r] counts request r's valid cached positions from the first; some request has exactly 4096.
All inputs are finite; a program needn't handle non-finite values.
Results may differ from a plain program's by a relative error of at most 0.012.
Values may be sent and summed in bfloat16 or wider, within the bound.
No kernel may reach another device: no remote copies, remote signals or barrier semaphores. Data moves between devices by JAX's collectives and lax.ppermute only.
A program may use at most 64 MiB of HBM per device.

v0:
```python
import jax
import jax.numpy as jnp
from jax import lax
from jax.sharding import PartitionSpec as P

H = 32
KVH = 8
HD = 128
norm_eps = 1e-06


def shards(
    queries,
    new_keys,
    new_values,
    cache_keys,
    cache_values,
    cache_len,
    residual,
    out_weight,
    norm_gain,
    gate_weight,
    up_weight,
    down_weight,
):
    n_mlp = lax.axis_size("mlp")
    heads_dev = H // n_mlp
    group_size = H // KVH
    kv_dev = max(1, heads_dev // group_size)
    per_kv = heads_dev // kv_dev
    query_rows = queries.shape[0]
    rows_dev = new_keys.shape[0]
    cache_total = cache_keys.shape[1] * n_mlp

    def to_slots(rows_block):
        row_count = rows_block.shape[0]
        copies = n_mlp // KVH
        spread = jnp.broadcast_to(
            rows_block.reshape(row_count, KVH, 1, HD), (row_count, KVH, copies, HD)
        )
        return spread.reshape(row_count, n_mlp, HD)

    arrived = (
        lax.all_to_all(to_slots(cache_keys[0]), "mlp", split_axis=1, concat_axis=0, tiled=True),
        lax.all_to_all(to_slots(cache_values[0]), "mlp", split_axis=1, concat_axis=0, tiled=True),
        lax.all_to_all(to_slots(new_keys), "mlp", split_axis=1, concat_axis=0, tiled=True),
        lax.all_to_all(to_slots(new_values), "mlp", split_axis=1, concat_axis=0, tiled=True),
    )
    keys_old = arrived[0]
    values_old = arrived[1]
    keys_new = arrived[2]
    values_new = arrived[3]
    grouped = queries.reshape(query_rows, kv_dev, per_kv, HD)
    score_scale = HD ** (-0.5)

    def absorb(running, key_part, value_part, allowed):
        row_max, row_sum, weighted = running
        scores = (
            jnp.einsum("tgqd,kgd->gqtk", grouped, key_part, preferred_element_type=jnp.float32)
            * score_scale
        )
        scores = jnp.where(allowed, scores, -jnp.inf)
        new_max = jnp.maximum(row_max, jnp.max(scores, axis=-1))
        shrink = jnp.exp(row_max - new_max)
        weights = jnp.exp(scores - new_max[..., None])
        row_sum = row_sum * shrink + jnp.sum(weights, axis=-1)
        weighted = weighted * shrink[..., None] + jnp.einsum(
            "gqtk,kgd->gqtd",
            weights.astype(jnp.bfloat16),
            value_part,
            preferred_element_type=jnp.float32,
        )
        return (new_max, row_sum, weighted)

    start_state = (
        jnp.full((kv_dev, per_kv, query_rows), -jnp.inf, jnp.float32),
        jnp.zeros((kv_dev, per_kv, query_rows), jnp.float32),
        jnp.zeros((kv_dev, per_kv, query_rows, HD), jnp.float32),
    )
    token_ids = lax.iota(jnp.int32, query_rows)
    causal = token_ids[None, :] <= token_ids[:, None]
    running = absorb(start_state, keys_new, values_new, causal)
    length = cache_len[0]
    key_block = min(512, cache_total)

    def visit(turn_index, running):
        offset = turn_index * key_block
        key_part = lax.dynamic_slice_in_dim(keys_old, offset, key_block, 0)
        value_part = lax.dynamic_slice_in_dim(values_old, offset, key_block, 0)
        positions = offset + lax.iota(jnp.int32, key_block)
        return absorb(running, key_part, value_part, (positions < length)[None, :])

    block_count = cache_total // key_block
    row_max, row_sum, weighted = lax.fori_loop(0, block_count, visit, running)
    attended = (weighted / row_sum[..., None]).astype(jnp.bfloat16)
    attended = attended.transpose(2, 0, 1, 3).reshape(query_rows, heads_dev * HD)
    partial_value = jnp.dot(attended, out_weight, preferred_element_type=jnp.float32)
    row_start = lax.axis_index("mlp") * rows_dev
    head_sum = lax.psum(partial_value.astype(jnp.bfloat16), "mlp").astype(jnp.float32)
    stream = (residual.astype(jnp.float32) + head_sum).astype(jnp.bfloat16)
    stream_full = stream.astype(jnp.float32)
    factor = lax.rsqrt(jnp.mean(stream_full * stream_full, axis=-1, keepdims=True) + norm_eps)
    normed = (stream_full * factor * norm_gain.astype(jnp.float32)).astype(jnp.bfloat16)
    stream_rows = lax.dynamic_slice_in_dim(stream, row_start, rows_dev, 0)
    gate_sum = jnp.dot(
        normed,
        lax.all_gather(gate_weight, "req", axis=0, tiled=True),
        preferred_element_type=jnp.float32,
    )
    up_sum = jnp.dot(
        normed,
        lax.all_gather(up_weight, "req", axis=0, tiled=True),
        preferred_element_type=jnp.float32,
    )
    hidden = (jax.nn.silu(gate_sum) * up_sum).astype(jnp.bfloat16)
    mlp_part = lax.dot_general(
        hidden,
        lax.all_gather(down_weight, "req", axis=0, tiled=True),
        (((1,), (1,)), ((), ())),
        preferred_element_type=jnp.float32,
    )
    mlp_rows = lax.psum_scatter(
        mlp_part.astype(jnp.bfloat16), "mlp", scatter_dimension=0, tiled=True
    ).astype(jnp.float32)
    return (stream_rows.astype(jnp.float32) + mlp_rows).astype(jnp.bfloat16)


def solution(mesh):
    in_specs = (
        P("req", "mlp"),
        P(("req", "mlp"), None),
        P(("req", "mlp"), None),
        P("req", "mlp", None),
        P("req", "mlp", None),
        P("req"),
        P("req", None),
        P("mlp", None),
        P(),
        P("req", "mlp"),
        P("req", "mlp"),
        P("req", "mlp"),
    )
    out_specs = P(("req", "mlp"), None)
    return jax.shard_map(shards, mesh=mesh, in_specs=in_specs, out_specs=out_specs, check_vma=False)
```

profile of v0, /device:TPU:2, one launch (start us, length us, event | category | flops | bytes accessed | tf_op | source)
XLA Modules:
  0.0 472.2 jit_solution(10438826310127697672)
XLA Ops:
  8.9 15.2 %all-to-all-start = ((bf16[24,16,128]{2,0,1:T(8,128)(2,1)}), bf16[24,16,128]{2,0,1:T(8,128)(2,1)S(1)}, u32[]{:S(2)}, u32[]{:S(2)}) async-start(bf16[24,16,128]{2,0,1:T(8,128)(2,1)} %bitcast.13), calls=%async_computation | async-start | bytes 196608 | tf_op jit(solution)/shard_map/all_to_all | solution.py:46
  25.0 12.7 %all-to-all-done = bf16[24,16,128]{2,0,1:T(8,128)(2,1)S(1)} async-done(((bf16[24,16,128]{2,0,1:T(8,128)(2,1)}), bf16[24,16,128]{2,0,1:T(8,128)(2,1)S(1)}, u32[]{:S(2)}, u32[]{:S(2)}) %all-to-all-start) | async-done | bytes 98336 | tf_op jit(solution)/shard_map/all_to_all | solution.py:46
  38.4 3.6 all-to-all-start.1
  43.2 11.9 %all-to-all-done.1 = bf16[24,16,128]{2,0,1:T(8,128)(2,1)S(1)} async-done(((bf16[24,16,128]{2,0,1:T(8,128)(2,1)}), bf16[24,16,128]{2,0,1:T(8,128)(2,1)S(1)}, u32[]{:S(2)}, u32[]{:S(2)}) %all-to-all-start.1) | async-done | bytes 98336 | tf_op jit(solution)/shard_map/all_to_all | solution.py:47
  56.3 3.7 all-to-all-start.2
  60.1 48.7 %all-to-all-done.2 = bf16[256,16,128]{2,0,1:T(8,128)(2,1)S(1)} async-done(((bf16[256,16,128]{2,0,1:T(8,128)(2,1)}), bf16[256,16,128]{2,0,1:T(8,128)(2,1)S(1)}, u32[]{:S(2)}, u32[]{:S(2)}) %all-to-all-start.2) | async-done | bytes 1048608 | tf_op jit(solution)/shard_map/all_to_all | solution.py:44
  108.9 1.3 broadcast_in_dim.100
  110.2 7.9 %all-to-all-start.3 = ((bf16[256,16,128]{2,0,1:T(8,128)(2,1)}), bf16[256,16,128]{2,0,1:T(8,128)(2,1)S(1)}, u32[]{:S(2)}, u32[]{:S(2)}) async-start(bf16[256,16,128]{2,0,1:T(8,128)(2,1)} %bitcast.35), calls=%async_computation.3 | async-start | bytes 2097152 | tf_op jit(solution)/shard_map/all_to_all | solution.py:45
  119.5 48.7 %all-to-all-done.3 = bf16[256,16,128]{2,0,1:T(8,128)(2,1)S(1)} async-done(((bf16[256,16,128]{2,0,1:T(8,128)(2,1)}), bf16[256,16,128]{2,0,1:T(8,128)(2,1)S(1)}, u32[]{:S(2)}, u32[]{:S(2)}) %all-to-all-start.3) | async-done | bytes 1048608 | tf_op jit(solution)/shard_map/all_to_all | solution.py:45
  168.2 22.4 %while.17 = (s32[]{:T(128)}, f32[1,2,384]{2,1,0:T(2,128)S(1)}, f32[1,2,384]{2,1,0:T(2,128)S(1)}, f32[1,2,384,128]{3,2,1,0:T(8,128)S(1)}, s32[]{:T(128)}, /*index...) while((s32[]{:T(128)}, f32[1,2,384]{2,1,0:T(2,128)S(1)}, ...), condition=%wide.region_5.6_spmd, body=%wide.region_2.5_spmd.sunk | while | flops 204279040 | bytes 6014131 | solution.py:94
  168.8 1.3 bitcast_reduce_fusion.2
  174.5 1.3 bitcast_reduce_fusion.2
  177.3 1.3 bitcast_reduce_fusion.2
  180.1 1.3 bitcast_reduce_fusion.2
  182.9 1.3 bitcast_reduce_fusion.2
  185.7 1.3 bitcast_reduce_fusion.2
  190.8 2.1 convolution_convert_fusion.1
  194.8 139.0 %all-reduce.2.cloned.1.call-done = bf16[384,2560]{1,0:T(8,128)(2,1)} async-done(((bf16[384,2560]{1,0:T(8,128)(2,1)}), bf16[384,2560]{1,0:T(8,128)(2,1)}) %all-reduce.2.cloned.1.call-update) | async-done | bytes 1966096 | tf_op jit(solution)/shard_map/psum | solution.py:99
  333.8 3.0 fusion.15
  336.8 4.8 %fusion.29 = f32[384,608]{0,1:T(8,128)} fusion(bf16[2560,608]{1,0:T(8,128)(2,1)} %all-gather.4.cloned.1.call-done, bf16[384,2560]{1,0:T(8,128)(2,1)S(1)} %get-tuple-element.174, f32[2560]{0:T(1024)S(1)} %convert_element_type.57, f32[384]{0:T(512)S(1)} %add_rsqrt_fusion), kind=kOutput, calls=%fused_computation.43 | convolution fusion | flops 1199308800 | bytes 6024704 | tf_op jit(solution)/shard_map/dot_general | solution.py:105
  341.6 40.2 %all-gather.8.cloned.1.call-done = bf16[2560,608]{1,0:T(8,128)(2,1)} async-done(((bf16[80,608]{1,0:T(8,128)(2,1)}), bf16[2560,608]{1,0:T(8,128)(2,1)}) %all-gather.8.cloned.1.call-update) | async-done | bytes 3112976 | tf_op jit(solution)/shard_map/all_gather | solution.py:118
  381.8 8.1 %convolution_convert_fusion = bf16[384,2560]{1,0:T(8,128)(2,1)} fusion(bf16[2560,608]{1,0:T(8,128)(2,1)} %all-gather.8.cloned.1.call-done, bf16[2560,608]{1,0:T(8,128)(2,1)} %all-gather.6.cloned.1.call-done, f32[384,608]{0,1:T(8,128)} %fusion.29, bf16[384,2560]{1,0:T(8,128)(2,1)S(1)} %get-tuple-element.174, f32[2560]{0:T(1024)S(1)} %convert_element_type.57, ...), kind=kOutput, calls=%fused_computation.24 | convolution fusion | flops 2397069312 | bytes 11103744 | tf_op jit(solution)/shard_map/dot_general | solution.py:116
  389.9 73.1 %reduce-scatter.2.cloned.1.call-done = bf16[24,2560]{1,0:T(8,128)(2,1)} async-done(((bf16[384,2560]{1,0:T(8,128)(2,1)}), bf16[24,2560]{1,0:T(8,128)(2,1)}) %reduce-scatter.2.cloned.1.call-update) | async-done | bytes 122896 | tf_op jit(solution)/shard_map/reduce_scatter | solution.py:122
  463.0 1.6 add_convert_fusion.1
  (93 shorter events, 23.2 us)
Async XLA Ops:
  7.4 183.5 %copy-start = (bf16[256,2560]{1,0:T(8,128)(2,1)S(1)}, bf16[256,2560]{1,0:T(8,128)(2,1)}, u32[]{:S(2)}) copy-start(bf16[256,2560]{1,0:T(8,128)(2,1)} %param.21) | copy-start | bytes 3932164
  8.9 28.8 %all-to-all-start = ((bf16[24,16,128]{2,0,1:T(8,128)(2,1)}), bf16[24,16,128]{2,0,1:T(8,128)(2,1)S(1)}, u32[]{:S(2)}, u32[]{:S(2)}) async-start(bf16[24,16,128]{2,0,1:T(8,128)(2,1)} %bitcast.13), calls=%async_computation | async-start | bytes 196608 | tf_op jit(solution)/shard_map/all_to_all | solution.py:46
  38.4 16.8 %all-to-all-start.1 = ((bf16[24,16,128]{2,0,1:T(8,128)(2,1)}), bf16[24,16,128]{2,0,1:T(8,128)(2,1)S(1)}, u32[]{:S(2)}, u32[]{:S(2)}) async-start(bf16[24,16,128]{2,0,1:T(8,128)(2,1)} %bitcast.23), calls=%async_computation.1 | async-start | bytes 196608 | tf_op jit(solution)/shard_map/all_to_all | solution.py:47
  43.2 16.8 %copy-start.2 = (bf16[1,256,1024]{2,1,0:T(8,128)(2,1)S(1)}, bf16[1,256,1024]{2,1,0:T(8,128)(2,1)}, u32[]{:S(2)}) copy-start(bf16[1,256,1024]{2,1,0:T(8,128)(2,1)} %param.18) | copy-start | bytes 1572868
  56.3 52.6 %all-to-all-start.2 = ((bf16[256,16,128]{2,0,1:T(8,128)(2,1)}), bf16[256,16,128]{2,0,1:T(8,128)(2,1)S(1)}, u32[]{:S(2)}, u32[]{:S(2)}) async-start(bf16[256,16,128]{2,0,1:T(8,128)(2,1)} %bitcast.30), calls=%async_computation.2 | async-start | bytes 2097152 | tf_op jit(solution)/shard_map/all_to_all | solution.py:44
  60.1 58.0 %copy-start.3 = (bf16[384,256]{1,0:T(8,128)(2,1)S(1)}, bf16[384,256]{1,0:T(8,128)(2,1)}, u32[]{:S(2)}) copy-start(bf16[384,256]{1,0:T(8,128)(2,1)} %param.14) | copy-start | bytes 589828
  108.8 1.3 copy-start.1
  110.2 58.0 %all-to-all-start.3 = ((bf16[256,16,128]{2,0,1:T(8,128)(2,1)}), bf16[256,16,128]{2,0,1:T(8,128)(2,1)S(1)}, u32[]{:S(2)}, u32[]{:S(2)}) async-start(bf16[256,16,128]{2,0,1:T(8,128)(2,1)} %bitcast.35), calls=%async_computation.3 | async-start | bytes 2097152 | tf_op jit(solution)/shard_map/all_to_all | solution.py:45
  118.1 215.7 %all-reduce.2.cloned.1.call-start = ((), (), s32[]{:S(2)}) async-start(), calls=%async_computation.5 | async-start | bytes 3932160 | tf_op jit(solution)/shard_map/psum | solution.py:99
  192.9 1.8 copy-start.4
  193.0 143.8 %all-gather.4.cloned.1.call-start = ((), (), s32[]{:S(2)}) async-start(), calls=%async_computation.6 | async-start | bytes 3379200 | tf_op jit(solution)/shard_map/all_gather | solution.py:107
  193.5 148.1 %all-gather.6.cloned.1.call-start = ((), (), s32[]{:S(2)}) async-start(), calls=%async_computation.7 | async-start | bytes 3379200 | tf_op jit(solution)/shard_map/all_gather | solution.py:112
  194.1 187.7 %all-gather.8.cloned.1.call-start = ((), (), s32[]{:S(2)}) async-start(), calls=%async_computation.8 | async-start | bytes 3379200 | tf_op jit(solution)/shard_map/all_gather | solution.py:118
  194.7 268.3 %reduce-scatter.2.cloned.1.call-start = ((), (), s32[]{:S(2)}) async-start(), calls=%async_computation.9 | async-start | bytes 2088960 | tf_op jit(solution)/shard_map/reduce_scatter | solution.py:122
Sparse Core Ops, SparseCore 0:
  193.1 140.6 all-reduce.1
  390.1 72.9 reduce-scatter.1
Sparse Core Ops, SparseCore 1:
  197.1 57.5 all-gather.3
  258.3 59.9 all-gather.5
  321.8 59.9 all-gather.7
where the time goes:
time: 473 us; the launch traced here: 472 us
  waiting for transfers between devices  376 us (79%)
  starting transfers between devices  30.5 us (6%)
  matrix products  30.4 us (6%)
  between operations  15.2 us (3%)
  other arithmetic  12.1 us (3%)
  local copies, waits for them, and re-layouts  7.44 us (2%)
    psum x1, waiting for transfers between devices, shards(): lax.psum(partial_value.astype(jnp.bfloat16), 'mlp').astype(jnp.float32)  139 us
    reduce_scatter x1, waiting for transfers between devices, shards(): lax.psum_scatter(mlp_part.astype(jnp.bfloat16), 'mlp', scatter_dimension=...  73.1 us
    all_to_all x1, waiting for transfers between devices, shards(): lax.all_to_all(to_slots(cache_keys[0]), 'mlp', split_axis=1, concat_axis=...  48.7 us
    all_to_all x1, waiting for transfers between devices, shards(): lax.all_to_all(to_slots(cache_values[0]), 'mlp', split_axis=1, concat_axi...  48.7 us
    all_gather x1, waiting for transfers between devices, shards(): lax.all_gather(down_weight, 'req', axis=0, tiled=True)  40.2 us
    all_to_all x1, starting transfers between devices, shards(): lax.all_to_all(to_slots(new_keys), 'mlp', split_axis=1, concat_axis=0, ti...  15.2 us
    all_to_all x1, waiting for transfers between devices, shards(): lax.all_to_all(to_slots(new_keys), 'mlp', split_axis=1, concat_axis=0, ti...  12.7 us
    all_to_all x1, waiting for transfers between devices, shards(): lax.all_to_all(to_slots(new_values), 'mlp', split_axis=1, concat_axis=0,...  11.9 us
  transfers between devices with their start and end apart: 9, of which 7 were waited for; matrix products, arithmetic and copies ran while one was open for 2% of the time, Pallas kernels for 0%

commit v1 on v0

--- a/solution.py
+++ b/solution.py
@@ -96,7 +96,9 @@
     attended = attended.transpose(2, 0, 1, 3).reshape(query_rows, heads_dev * HD)
     partial_value = jnp.dot(attended, out_weight, preferred_element_type=jnp.float32)
     row_start = lax.axis_index("mlp") * rows_dev
-    head_sum = lax.psum(partial_value.astype(jnp.bfloat16), "mlp").astype(jnp.float32)
+    head_sum = jnp.sum(lax.all_gather(partial_value.astype(jnp.bfloat16), "mlp"), axis=0).astype(
+        jnp.float32
+    )
     stream = (residual.astype(jnp.float32) + head_sum).astype(jnp.bfloat16)
     stream_full = stream.astype(jnp.float32)
     factor = lax.rsqrt(jnp.mean(stream_full * stream_full, axis=-1, keepdims=True) + norm_eps)

time: 473 us -> 805 us (1.70)
  the two profiles are of different devices: /device:TPU:2 before, /device:TPU:6 now
where the time goes in v1:
time: 805 us; the launch traced here: 804 us
  waiting for transfers between devices  697 us (87%)
  matrix products  31.1 us (4%)
  starting transfers between devices  30.7 us (4%)
  other arithmetic  24.1 us (3%)
  between operations  13.4 us (2%)
    all_gather x1, waiting for transfers between devices, shards(): lax.all_gather(partial_value.astype(jnp.bfloat16), 'mlp')  333 us
    reduce_scatter x1, waiting for transfers between devices, shards(): lax.psum_scatter(mlp_part.astype(jnp.bfloat16), 'mlp', scatter_dimension=...  73 us
    all_gather x1, waiting for transfers between devices, shards(): lax.all_gather(up_weight, 'req', axis=0, tiled=True)  63.2 us
    all_gather x1, waiting for transfers between devices, shards(): lax.all_gather(down_weight, 'req', axis=0, tiled=True)  57.9 us
    all_to_all x1, waiting for transfers between devices, shards(): lax.all_to_all(to_slots(cache_keys[0]), 'mlp', split_axis=1, concat_axis=...  48.7 us
    all_to_all x1, waiting for transfers between devices, shards(): lax.all_to_all(to_slots(cache_values[0]), 'mlp', split_axis=1, concat_axi...  48.7 us
    all_gather x1, waiting for transfers between devices, shards(): lax.all_gather(gate_weight, 'req', axis=0, tiled=True)  46.3 us
  transfers between devices with their start and end apart: 9, of which 9 were waited for; matrix products, arithmetic and copies ran while one was open for 3% of the time, Pallas kernels for 0%

profile of v1, /device:TPU:6, one launch (start us, length us, event | category | flops | bytes accessed | tf_op | source)
XLA Modules:
  0.0 804.1 jit_solution(17050621892659843315)
XLA Ops:
  8.1 15.2 %all-to-all-start = ((bf16[24,16,128]{2,0,1:T(8,128)(2,1)}), bf16[24,16,128]{2,0,1:T(8,128)(2,1)S(1)}, u32[]{:S(2)}, u32[]{:S(2)}) async-start(bf16[24,16,128]{2,0,1:T(8,128)(2,1)} %bitcast.13), calls=%async_computation | async-start | bytes 196608 | tf_op jit(solution)/shard_map/all_to_all | solution.py:46
  24.1 12.7 %all-to-all-done = bf16[24,16,128]{2,0,1:T(8,128)(2,1)S(1)} async-done(((bf16[24,16,128]{2,0,1:T(8,128)(2,1)}), bf16[24,16,128]{2,0,1:T(8,128)(2,1)S(1)}, u32[]{:S(2)}, u32[]{:S(2)}) %all-to-all-start) | async-done | bytes 98336 | tf_op jit(solution)/shard_map/all_to_all | solution.py:46
  37.5 3.6 all-to-all-start.1
  42.3 11.9 %all-to-all-done.1 = bf16[24,16,128]{2,0,1:T(8,128)(2,1)S(1)} async-done(((bf16[24,16,128]{2,0,1:T(8,128)(2,1)}), bf16[24,16,128]{2,0,1:T(8,128)(2,1)S(1)}, u32[]{:S(2)}, u32[]{:S(2)}) %all-to-all-start.1) | async-done | bytes 98336 | tf_op jit(solution)/shard_map/all_to_all | solution.py:47
  55.5 3.7 all-to-all-start.2
  59.3 48.7 %all-to-all-done.2 = bf16[256,16,128]{2,0,1:T(8,128)(2,1)S(1)} async-done(((bf16[256,16,128]{2,0,1:T(8,128)(2,1)}), bf16[256,16,128]{2,0,1:T(8,128)(2,1)S(1)}, u32[]{:S(2)}, u32[]{:S(2)}) %all-to-all-start.2) | async-done | bytes 1048608 | tf_op jit(solution)/shard_map/all_to_all | solution.py:44
  108.0 1.3 broadcast_in_dim.100
  109.3 7.9 all-to-all-start.3
  118.7 48.7 %all-to-all-done.3 = bf16[256,16,128]{2,0,1:T(8,128)(2,1)S(1)} async-done(((bf16[256,16,128]{2,0,1:T(8,128)(2,1)}), bf16[256,16,128]{2,0,1:T(8,128)(2,1)S(1)}, u32[]{:S(2)}, u32[]{:S(2)}) %all-to-all-start.3) | async-done | bytes 1048608 | tf_op jit(solution)/shard_map/all_to_all | solution.py:45
  167.3 22.4 %while.17 = (s32[]{:T(128)}, f32[1,2,384]{2,1,0:T(2,128)S(1)}, f32[1,2,384]{2,1,0:T(2,128)S(1)}, f32[1,2,384,128]{3,2,1,0:T(8,128)S(1)}, s32[]{:T(128)}, /*index...) while((s32[]{:T(128)}, f32[1,2,384]{2,1,0:T(2,128)S(1)}, ...), condition=%wide.region_5.6_spmd, body=%wide.region_2.5_spmd.sunk | while | flops 204279040 | bytes 6014131 | solution.py:94
  168.0 1.3 bitcast_reduce_fusion.2
  170.8 1.3 bitcast_reduce_fusion.2
  173.6 1.3 bitcast_reduce_fusion.2
  190.0 2.0 convolution_convert_fusion.1
  194.4 332.7 %all-gather.12.cloned.1.call-done = bf16[6144,2560]{1,0:T(8,128)(2,1)} async-done(((bf16[384,2560]{1,0:T(8,128)(2,1)}), bf16[6144,2560]{1,0:T(8,128)(2,1)}) %all-gather.12.cloned.1.call-update) | async-done | bytes 31457296 | tf_op jit(solution)/shard_map/all_gather | solution.py:99
  527.0 11.3 %reduce_sum.47 = bf16[384,2560]{1,0:T(8,128)(2,1)S(1)} reduce(bf16[16,384,2560]{2,1,0:T(8,128)(2,1)} %bitcast.148, bf16[]{:T(256)} %constant.68.clone.1), dimensions={0}, to_apply=%region_6.7 | reduce | flops 14745600 | bytes 33423362 | tf_op jit(solution)/shard_map/reduce_sum | solution.py:99
  538.3 3.7 fusion.15
  542.0 46.3 %all-gather.6.cloned.1.call-done = bf16[2560,608]{1,0:T(8,128)(2,1)} async-done(((bf16[80,608]{1,0:T(8,128)(2,1)}), bf16[2560,608]{1,0:T(8,128)(2,1)}) %all-gather.6.cloned.1.call-update) | async-done | bytes 3112976 | tf_op jit(solution)/shard_map/all_gather | solution.py:109
  588.3 5.5 fusion.29
  593.8 57.9 %all-gather.10.cloned.1.call-done = bf16[2560,608]{1,0:T(8,128)(2,1)} async-done(((bf16[80,608]{1,0:T(8,128)(2,1)}), bf16[2560,608]{1,0:T(8,128)(2,1)}) %all-gather.10.cloned.1.call-update) | async-done | bytes 3112976 | tf_op jit(solution)/shard_map/all_gather | solution.py:120
  651.7 63.2 %all-gather.8.cloned.1.call-done = bf16[2560,608]{1,0:T(8,128)(2,1)} async-done(((bf16[80,608]{1,0:T(8,128)(2,1)}), bf16[2560,608]{1,0:T(8,128)(2,1)}) %all-gather.8.cloned.1.call-update) | async-done | bytes 3112976 | tf_op jit(solution)/shard_map/all_gather | solution.py:114
  714.9 8.1 %convolution_convert_fusion = bf16[384,2560]{1,0:T(8,128)(2,1)} fusion(bf16[2560,608]{1,0:T(8,128)(2,1)} %all-gather.10.cloned.1.call-done, bf16[2560,608]{1,0:T(8,128)(2,1)} %all-gather.8.cloned.1.call-done, f32[384,608]{0,1:T(8,128)} %fusion.29, bf16[384,2560]{1,0:T(8,128)(2,1)S(1)} %copy-done.2, f32[2560]{0:T(1024)S(1)} %convert_element_type.59, ...), kind=kOutput, calls=%fused_computation.24 | convolution fusion | flops 2397069312 | bytes 11103744 | tf_op jit(solution)/shard_map/dot_general | solution.py:118
  723.1 73.0 %reduce-scatter.2.cloned.1.call-done = bf16[24,2560]{1,0:T(8,128)(2,1)} async-done(((bf16[384,2560]{1,0:T(8,128)(2,1)}), bf16[24,2560]{1,0:T(8,128)(2,1)}) %reduce-scatter.2.cloned.1.call-update) | async-done | bytes 122896 | tf_op jit(solution)/shard_map/reduce_scatter | solution.py:124
  796.0 1.6 add_convert_fusion.1
  (96 shorter events, 27.6 us)
Async XLA Ops:
  6.5 183.5 %copy-start = (bf16[256,2560]{1,0:T(8,128)(2,1)S(1)}, bf16[256,2560]{1,0:T(8,128)(2,1)}, u32[]{:S(2)}) copy-start(bf16[256,2560]{1,0:T(8,128)(2,1)} %param.21) | copy-start | bytes 3932164
  8.1 28.8 %all-to-all-start = ((bf16[24,16,128]{2,0,1:T(8,128)(2,1)}), bf16[24,16,128]{2,0,1:T(8,128)(2,1)S(1)}, u32[]{:S(2)}, u32[]{:S(2)}) async-start(bf16[24,16,128]{2,0,1:T(8,128)(2,1)} %bitcast.13), calls=%async_computation | async-start | bytes 196608 | tf_op jit(solution)/shard_map/all_to_all | solution.py:46
  37.5 16.8 %all-to-all-start.1 = ((bf16[24,16,128]{2,0,1:T(8,128)(2,1)}), bf16[24,16,128]{2,0,1:T(8,128)(2,1)S(1)}, u32[]{:S(2)}, u32[]{:S(2)}) async-start(bf16[24,16,128]{2,0,1:T(8,128)(2,1)} %bitcast.23), calls=%async_computation.1 | async-start | bytes 196608 | tf_op jit(solution)/shard_map/all_to_all | solution.py:47
  42.3 16.8 %copy-start.3 = (bf16[1,256,1024]{2,1,0:T(8,128)(2,1)S(1)}, bf16[1,256,1024]{2,1,0:T(8,128)(2,1)}, u32[]{:S(2)}) copy-start(bf16[1,256,1024]{2,1,0:T(8,128)(2,1)} %param.18) | copy-start | bytes 1572868
  55.5 52.6 %all-to-all-start.2 = ((bf16[256,16,128]{2,0,1:T(8,128)(2,1)}), bf16[256,16,128]{2,0,1:T(8,128)(2,1)S(1)}, u32[]{:S(2)}, u32[]{:S(2)}) async-start(bf16[256,16,128]{2,0,1:T(8,128)(2,1)} %bitcast.30), calls=%async_computation.2 | async-start | bytes 2097152 | tf_op jit(solution)/shard_map/all_to_all | solution.py:44
  59.3 58.0 %copy-start.4 = (bf16[384,256]{1,0:T(8,128)(2,1)S(1)}, bf16[384,256]{1,0:T(8,128)(2,1)}, u32[]{:S(2)}) copy-start(bf16[384,256]{1,0:T(8,128)(2,1)} %param.14) | copy-start | bytes 589828
  108.0 1.3 copy-start.1
  109.3 58.0 %all-to-all-start.3 = ((bf16[256,16,128]{2,0,1:T(8,128)(2,1)}), bf16[256,16,128]{2,0,1:T(8,128)(2,1)S(1)}, u32[]{:S(2)}, u32[]{:S(2)}) async-start(bf16[256,16,128]{2,0,1:T(8,128)(2,1)} %bitcast.35), calls=%async_computation.3 | async-start | bytes 2097152 | tf_op jit(solution)/shard_map/all_to_all | solution.py:45
  117.2 409.8 %all-gather.12.cloned.1.call-start = ((), (), s32[]{:S(2)}) async-start(), calls=%async_computation.9 | async-start | bytes 33423360 | tf_op jit(solution)/shard_map/all_gather | solution.py:99
  192.0 2.3 copy-start.5
  192.0 396.3 %all-gather.6.cloned.1.call-start = ((), (), s32[]{:S(2)}) async-start(), calls=%async_computation.5 | async-start | bytes 3379200 | tf_op jit(solution)/shard_map/all_gather | solution.py:109
  192.8 458.9 %all-gather.10.cloned.1.call-start = ((), (), s32[]{:S(2)}) async-start(), calls=%async_computation.7 | async-start | bytes 3379200 | tf_op jit(solution)/shard_map/all_gather | solution.py:120
  193.5 521.4 %all-gather.8.cloned.1.call-start = ((), (), s32[]{:S(2)}) async-start(), calls=%async_computation.6 | async-start | bytes 3379200 | tf_op jit(solution)/shard_map/all_gather | solution.py:114
  194.1 601.9 %reduce-scatter.2.cloned.1.call-start = ((), (), s32[]{:S(2)}) async-start(), calls=%async_computation.8 | async-start | bytes 2088960 | tf_op jit(solution)/shard_map/reduce_scatter | solution.py:124
  588.3 126.6 %copy-start.2 = (bf16[384,2560]{1,0:T(8,128)(2,1)S(1)}, bf16[384,2560]{1,0:T(8,128)(2,1)}, u32[]{:S(2)}) copy-start(bf16[384,2560]{1,0:T(8,128)(2,1)} %get-tuple-element.174) | copy-start | bytes 5898244
Sparse Core Ops, SparseCore 0:
  192.2 334.8 all-gather.11
  530.2 58.0 all-gather.5
  591.5 60.1 all-gather.9
  654.7 60.1 all-gather.7
  723.2 72.8 reduce-scatter.1
